TPU v7x, 256 devices: a whole 4x4x8 slice. The times are simulated.
256 devices in a mesh: section: 16 (over z_lo, y, core), tensor: 16 (over x, z_hi).
Axes of the slice: x: 4, y: 4, z: 8 (z_hi: 4, z_lo: 2; z = z_hi * 2 + z_lo), core: 2. Of those that a mesh axis runs over, the one named last changes fastest.
Arguments:
- hidden: bfloat16 [16, 64, 8192], P('section'), may hold values from -14 to 14
- head: bfloat16 [8192, 65536], P('section', 'tensor'), may hold values from -0.25 to 0.25
- exit_loss_weight: float32 [16], P('section'), may hold values from 2 to 32
Outputs:
- grad_hidden: float32 [1024, 8192], P('tensor', 'section')
- grad_head: bfloat16 [8192, 65536], P('section', 'tensor')
All inputs are finite; a program needn't handle non-finite values.
Results may differ from a plain program's by a relative error of at most 0.011.
Values may be sent and summed in bfloat16 or wider, within the bound.
No kernel may reach another device: no remote copies, remote signals or barrier semaphores. Data moves between devices by JAX's collectives and lax.ppermute only.
A program may use at most 128 MiB of HBM per device.

v0:
```python
import jax
import jax.numpy as jnp
import numpy as np
from jax import lax
from jax.sharding import Mesh
from jax.sharding import PartitionSpec as P

scaling_divisor = 2.0
SEC = ("pair", "core")


def _lse(x, axes):
    top = jnp.max(x, axis=axes, keepdims=True)
    return top + jnp.log(jnp.sum(jnp.exp(x - top), axis=axes, keepdims=True))


def local(hidden, head, exit_loss_weight):
    pairs = lax.axis_size("pair")
    sections = pairs * 2
    tensors = lax.axis_size("tensor")
    _, tok, width = hidden.shape
    exits = sections
    dblk = width // sections
    vblk = head.shape[1]
    tps = tok // sections
    n_eq = tensors // tps
    kpe = exits // n_eq
    partner_head = lax.ppermute(head, "core", perm=[(0, 1), (1, 0)])
    head_pair = jnp.concatenate([head, partner_head], axis=0)
    h6 = hidden[0].reshape(pairs, 2, tps, pairs, 2, dblk)
    a = h6.transpose(3, 1, 0, 2, 4, 5)
    fwd = jnp.stack([a[:, 0], a[:, 1, :, :, ::-1, :]], axis=1)
    full = hidden[0].reshape(tok, sections, dblk).transpose(1, 0, 2)
    send = jnp.stack([fwd.reshape(sections, -1), full.reshape(sections, -1)], axis=1)
    recv = lax.all_to_all(send, SEC, 0, 0, tiled=True)
    cols = recv[:, 1].reshape(exits, tok, dblk)
    lhs = recv[:, 0].reshape(exits, pairs, tps, 2 * dblk).transpose(1, 0, 2, 3)
    lhs = lhs.reshape(pairs * exits * tps, 2 * dblk)
    part = jnp.dot(lhs, head_pair, preferred_element_type=jnp.float32)
    part, w_local = lax.optimization_barrier((part, exit_loss_weight))
    weights = lax.all_gather(w_local, SEC, axis=0, tiled=True)
    own = lax.psum_scatter(part, "pair", scatter_dimension=0, tiled=True)
    own, weights = lax.optimization_barrier((own, weights))
    own = own.reshape(n_eq, kpe, tps, vblk)
    stud = own.transpose(2, 0, 1, 3).reshape(tensors, kpe, vblk)
    teach = jnp.broadcast_to(own[n_eq - 1, kpe - 1][:, None, None, :], (tps, n_eq, 1, vblk))
    send2 = jnp.concatenate([stud, teach.reshape(tensors, 1, vblk)], axis=1)
    rows = lax.all_to_all(send2, "tensor", 0, 0, tiled=True)
    logits = rows[:, :kpe, :]
    teacher = rows[:, kpe, :] / scaling_divisor
    log_student = logits - _lse(logits, (0, 2))
    log_teacher = teacher - _lse(teacher, (0, 1))
    log_mixture = jnp.logaddexp(log_student, log_teacher[:, None, :]) - jnp.log(2.0)
    halfgap = 0.5 * (log_student - log_mixture)
    student = jnp.exp(log_student)
    average = jnp.sum(student * halfgap, axis=(0, 2), keepdims=True)
    eq = lax.rem(lax.axis_index("tensor"), n_eq)
    wk = lax.dynamic_slice(weights, (eq * kpe,), (kpe,))
    grad_logits = (wk[None, :, None] * student * (halfgap - average)).astype(jnp.bfloat16)
    back = lax.all_to_all(grad_logits, "tensor", 0, 0, tiled=True)
    back = back.reshape(tps, exits, vblk)
    piece = lax.all_gather(back, SEC, axis=0, tiled=True)
    head_grad = lax.dot_general(
        cols, piece, (((0, 1), (1, 0)), ((), ())), preferred_element_type=jnp.float32
    )
    row_grad = lax.dot_general(
        piece, head, (((2,), (1,)), ((), ())), preferred_element_type=jnp.float32
    )
    grad_hidden = lax.psum_scatter(row_grad, "tensor", scatter_dimension=1, tiled=True)
    grad_hidden = grad_hidden.reshape(tok, dblk)
    return (grad_hidden, head_grad.astype(jnp.bfloat16))


def solution(mesh):
    shape = mesh.devices.shape
    inner = Mesh(
        np.asarray(mesh.devices).reshape(shape[0] // 2, 2, shape[1]), ("pair", "core", "tensor")
    )
    placed = (P(SEC, None, None), P(SEC, "tensor"), P(SEC))
    return jax.shard_map(
        local,
        mesh=inner,
        in_specs=placed,
        out_specs=(P("tensor", SEC), P(SEC, "tensor")),
        check_vma=False,
    )
```

profile of v0, /device:TPU:8, one launch (start us, length us, event | category | flops | bytes accessed | tf_op | source)
XLA Modules:
  0.0 433.1 jit_solution(12043793999282986412)
XLA Ops:
  7.2 1.8 reshape_squeeze.12
  9.0 1.0 copy.41
  10.0 1.8 fusion.12
  11.8 2.8 rev.3
  14.5 2.5 pad_maximum_fusion.2
  17.1 0.8 stack_reshape.6
  19.6 3.5 copy.25
  23.1 6.3 %all-to-all-start = ((bf16[16,2,32768]{2,1,0:T(2,128)(2,1)}), bf16[16,2,32768]{2,1,0:T(2,128)(2,1)S(1)}, u32[]{:S(2)}, u32[]{:S(2)}) async-start(bf16[16,2,32768]{2,1,0:T(2,128)(2,1)} %copy.25), calls=%async_computation | async-start | bytes 4194304 | tf_op jit(solution)/shard_map/all_to_all | solution.py:35
  29.4 0.7 collective-permute-start
  30.1 26.8 %all-to-all-done = bf16[16,2,32768]{2,1,0:T(2,128)(2,1)S(1)} async-done(((bf16[16,2,32768]{2,1,0:T(2,128)(2,1)}), bf16[16,2,32768]{2,1,0:T(2,128)(2,1)S(1)}, u32[]{:S(2)}, u32[]{:S(2)}) %all-to-all-start) | async-done | bytes 2097184 | tf_op jit(solution)/shard_map/all_to_all | solution.py:35
  56.9 10.0 %slice_reduce_fusion = (bf16[16,32768]{1,0:T(8,128)(2,1)S(1)}, bf16[16,32768]{1,0:T(8,128)(2,1)}) fusion(bf16[16,2,32768]{2,1,0:T(2,128)(2,1)S(1)} %all-to-all-done), kind=kLoop, calls=%fused_computation.9 | loop fusion | bytes 4194304 | tf_op jit(solution)/shard_map/slice | solution.py:36
  66.8 1.8 reshape_squeeze.14
  69.4 11.2 %fusion = f32[512,4096]{1,0:T(8,128)} fusion(bf16[512,1024]{1,0:T(8,128)(2,1)S(1)} %reshape.46, bf16[512,4096]{1,0:T(8,128)(2,1)} %collective-permute-done, bf16[512,4096]{1,0:T(8,128)(2,1)} %param.4), kind=kOutput, calls=%fused_computation | convolution fusion | flops 4311744512 | bytes 17825792 | tf_op jit(solution)/shard_map/dot_general | solution.py:39
  81.9 0.8 dynamic-update-slice
  82.6 29.3 %all-reduce = f32[16]{0:T(128)S(1)} all-reduce(f32[16]{0:T(128)S(1)} %dynamic-update-slice), channel_id=1, replica_groups=mesh['pair'=8,'core'=2,'tensor'=16] {'pair','core'}, use_global_device_ids=true, to_apply=%add | all-reduce | flops 16 | bytes 128 | tf_op jit(solution)/shard_map/optimization_barrier | solution.py:43
  112.0 65.4 %reduce-scatter.3.cloned.1.call-done = f32[64,4096]{1,0:T(8,128)} async-done(((f32[512,4096]{1,0:T(8,128)}), f32[64,4096]{1,0:T(8,128)}) %reduce-scatter.3.cloned.1.call-update) | async-done | bytes 1048592 | tf_op jit(solution)/shard_map/reduce_scatter | solution.py:42
  177.4 1.5 reshape.47
  179.0 0.7 copy.27
  180.1 1.7 pad_maximum_fusion.1
  181.8 9.5 %all-to-all-start.1 = ((f32[16,5,4096]{2,1,0:T(8,128)}), f32[16,5,4096]{2,1,0:T(8,128)S(1)}, u32[]{:S(2)}, u32[]{:S(2)}) async-start(f32[16,5,4096]{2,1,0:T(8,128)} %pad_maximum_fusion.1), calls=%async_computation.2 | async-start | bytes 4194304 | tf_op jit(solution)/shard_map/all_to_all | solution.py:48
  191.6 51.3 %all-to-all-done.1 = f32[16,5,4096]{2,1,0:T(8,128)S(1)} async-done(((f32[16,5,4096]{2,1,0:T(8,128)}), f32[16,5,4096]{2,1,0:T(8,128)S(1)}, u32[]{:S(2)}, u32[]{:S(2)}) %all-to-all-start.1) | async-done | bytes 1310752 | tf_op jit(solution)/shard_map/all_to_all | solution.py:48
  242.9 1.1 fusion.11
  244.0 1.8 exponential_reduce_fusion.1
  248.3 0.7 exponential_reduce_fusion
  249.1 2.2 multiply_reduce_fusion
  251.9 22.2 %all_to_all.15 = bf16[16,4,4096]{2,1,0:T(4,128)(2,1)S(1)} all-to-all(bf16[16,4,4096]{2,1,0:T(4,128)(2,1)S(1)} %multiply_convert_fusion), channel_id=1, replica_groups=mesh['pair'=8,'core'=2,'tensor'=16] {'tensor'}, dimensions={0} | all-to-all | bytes 1048576 | tf_op jit(solution)/shard_map/all_to_all | solution.py:60
  274.1 0.9 reshape.49
  275.1 50.5 %all-gather.2.cloned.1.call-done = bf16[64,16,4096]{2,1,0:T(8,128)(2,1)} async-done(((bf16[4,16,4096]{2,1,0:T(8,128)(2,1)}), bf16[64,16,4096]{2,1,0:T(8,128)(2,1)}) %all-gather.2.cloned.1.call-update) | async-done | bytes 8388624 | tf_op jit(solution)/shard_map/all_gather | solution.py:62
  325.6 8.2 %fusion.8 = f32[64,16,512]{2,1,0:T(8,128)S(1)} fusion(bf16[64,16,4096]{2,1,0:T(8,128)(2,1)} %all-gather.2.cloned.1.call-done, bf16[512,4096]{1,0:T(8,128)(2,1)} %param.4), kind=kOutput, calls=%fused_computation.7 | convolution fusion | flops 4294967296 | bytes 14680064 | tf_op jit(solution)/shard_map/dot_general | solution.py:66
  333.9 2.6 copy.28
  336.8 25.0 %bitcast_convert_fusion = bf16[512,4096]{1,0:T(8,128)(2,1)} fusion(bf16[16,64,512]{2,1,0:T(8,128)(2,1)S(1)} %bitcast.38, bf16[64,16,4096]{2,1,0:T(8,128)(2,1)} %all-gather.2.cloned.1.call-done), kind=kOutput, calls=%fused_computation.4 | convolution fusion | flops 4297064448 | bytes 13631488 | tf_op jit(solution)/shard_map/dot_general | solution.py:63
  361.8 64.6 %reduce-scatter.5.cloned.1.call-done = f32[64,1,512]{2,0,1:T(8,128)} async-done(((f32[64,16,512]{2,0,1:T(8,128)}), f32[64,1,512]{2,0,1:T(8,128)}) %reduce-scatter.5.cloned.1.call-update) | async-done | bytes 131088 | tf_op jit(solution)/shard_map/reduce_scatter | solution.py:69
  (29 shorter events, 5.8 us)
Async XLA Ops:
  10.0 7.9 %copy-start = (bf16[1,64,8192]{2,1,0:T(8,128)(2,1)S(1)}, bf16[1,64,8192]{2,1,0:T(8,128)(2,1)}, u32[]{:S(2)}) copy-start(bf16[1,64,8192]{2,1,0:T(8,128)(2,1)} %param.3) | copy-start | bytes 3145732
  23.1 33.8 %all-to-all-start = ((bf16[16,2,32768]{2,1,0:T(2,128)(2,1)}), bf16[16,2,32768]{2,1,0:T(2,128)(2,1)S(1)}, u32[]{:S(2)}, u32[]{:S(2)}) async-start(bf16[16,2,32768]{2,1,0:T(2,128)(2,1)} %copy.25), calls=%async_computation | async-start | bytes 4194304 | tf_op jit(solution)/shard_map/all_to_all | solution.py:35
  29.4 148.1 %reduce-scatter.3.cloned.1.call-start = ((), (), s32[]{:S(2)}) async-start(), calls=%async_computation.5 | async-start | bytes 9437184 | tf_op jit(solution)/shard_map/reduce_scatter | solution.py:42
  29.4 40.0 %collective-permute-start = (bf16[512,4096]{1,0:T(8,128)(2,1)}, bf16[512,4096]{1,0:T(8,128)(2,1)}, u32[]{:S(2)}, u32[]{:S(2)}) collective-permute-start(bf16[512,4096]{1,0:T(8,128)(2,1)} %param.4), channel_id=1, source_target_pairs={{0,16},{16,0},{1,17},{17,1},{2,18},{18,2},{3,19},{19,3},{4,20},{20... | collective-permute-start | bytes 12582920 | tf_op jit(solution)/shard_map/ppermute | solution.py:28
  80.6 0.7 copy-start.1
  181.8 61.1 %all-to-all-start.1 = ((f32[16,5,4096]{2,1,0:T(8,128)}), f32[16,5,4096]{2,1,0:T(8,128)S(1)}, u32[]{:S(2)}, u32[]{:S(2)}) async-start(f32[16,5,4096]{2,1,0:T(8,128)} %pad_maximum_fusion.1), calls=%async_computation.2 | async-start | bytes 4194304 | tf_op jit(solution)/shard_map/all_to_all | solution.py:48
  191.3 134.3 %all-gather.2.cloned.1.call-start = ((), (), s32[]{:S(2)}) async-start(), calls=%async_computation.6 | async-start | bytes 8912896 | tf_op jit(solution)/shard_map/all_gather | solution.py:62
  275.1 151.3 %reduce-scatter.5.cloned.1.call-start = ((), (), s32[]{:S(2)}) async-start(), calls=%async_computation.7 | async-start | bytes 2228224 | tf_op jit(solution)/shard_map/reduce_scatter | solution.py:69
Sparse Core Ops, SparseCore 0:
  80.8 96.6 reduce-scatter.2
  275.2 50.4 all-gather.1
  336.6 89.7 reduce-scatter.4
where the time goes:
time: 440 us; the launch traced here: 433 us
  waiting for transfers between devices  259 us (59%)
  blocking collectives  51.5 us (12%)
  matrix products  44.4 us (10%)
  local copies, waits for them, and re-layouts  33.6 us (8%)
  starting transfers between devices  16.8 us (4%)
  between operations  16.2 us (4%)
  other arithmetic  12 us (3%)
    reduce_scatter x1, waiting for transfers between devices, local(): own = lax.psum_scatter(part, 'pair', scatter_dimension=0, tiled=True)  65.4 us
    reduce_scatter x1, waiting for transfers between devices, local(): lax.psum_scatter(row_grad, 'tensor', scatter_dimension=1, tiled=True)  64.6 us
    all_to_all x1, waiting for transfers between devices, local(): rows = lax.all_to_all(send2, 'tensor', 0, 0, tiled=True)  51.3 us
    all_gather x1, waiting for transfers between devices, local(): piece = lax.all_gather(back, SEC, axis=0, tiled=True)  50.5 us
    optimization_barrier x1, blocking collectives, local(): own, weights = lax.optimization_barrier((own, weights))  29.3 us
    all_to_all x1, waiting for transfers between devices, local(): recv = lax.all_to_all(send, SEC, 0, 0, tiled=True)  26.8 us
    dot_general x1, matrix products, local(): lax.dot_general(cols, piece, (((0, 1), (1, 0)), ((), ())), preferred_elem...  25 us
    all_to_all x1, blocking collectives, local(): back = lax.all_to_all(grad_logits, 'tensor', 0, 0, tiled=True)  22.2 us
  transfers between devices with their start and end apart: 6, of which 5 were waited for; matrix products, arithmetic and copies ran while one was open for 9% of the time, Pallas kernels for 0%

commit v1 on v0

--- a/solution.py
+++ b/solution.py
@@ -59,7 +59,8 @@
     grad_logits = (wk[None, :, None] * student * (halfgap - average)).astype(jnp.bfloat16)
     back = lax.all_to_all(grad_logits, "tensor", 0, 0, tiled=True)
     back = back.reshape(tps, exits, vblk)
-    piece = lax.all_gather(back, SEC, axis=0, tiled=True)
+    sent = jnp.stack([back] * lax.axis_size(SEC))
+    piece = jnp.concatenate(lax.all_to_all(sent, SEC, 0, 0), axis=0)
     head_grad = lax.dot_general(
         cols, piece, (((0, 1), (1, 0)), ((), ())), preferred_element_type=jnp.float32
     )

time: 440 us -> 479 us (1.089)
  blocking collectives: 51.5 us -> 149 us
  waiting for transfers between devices: 259 us -> 203 us
    all_to_all x0 -> x1, blocking collectives: none -> 97.8 us  [local(): piece = jnp.concatenate(lax.all_to_all(sent, SEC, 0, 0), axis=0)]
    all_gather x1 -> x0, waiting for transfers between devices: 50.5 us -> none  [local(): piece = lax.all_gather(back, SEC, axis=0, tiled=True)]
  transfers between devices with their start and end apart: 6 -> 5, of which waited for: 5 -> 4; matrix products, arithmetic and copies ran while one was open for 9% -> 8% of each run, Pallas kernels for 0% -> 0%
where the time goes in v1:
time: 479 us; the launch traced here: 472 us
  waiting for transfers between devices  203 us (42%)
  blocking collectives  149 us (31%)
  matrix products  40.7 us (8%)
  local copies, waits for them, and re-layouts  34.4 us (7%)
  starting transfers between devices  16.7 us (3%)
  between operations  16.5 us (3%)
  other arithmetic  10.9 us (2%)
    all_to_all x1, blocking collectives, local(): piece = jnp.concatenate(lax.all_to_all(sent, SEC, 0, 0), axis=0)  97.8 us
    reduce_scatter x1, waiting for transfers between devices, local(): own = lax.psum_scatter(part, 'pair', scatter_dimension=0, tiled=True)  65.4 us
    reduce_scatter x1, waiting for transfers between devices, local(): lax.psum_scatter(row_grad, 'tensor', scatter_dimension=1, tiled=True)  59.8 us
    all_to_all x1, waiting for transfers between devices, local(): rows = lax.all_to_all(send2, 'tensor', 0, 0, tiled=True)  51.3 us
    optimization_barrier x1, blocking collectives, local(): own, weights = lax.optimization_barrier((own, weights))  29.3 us
    all_to_all x1, waiting for transfers between devices, local(): recv = lax.all_to_all(send, SEC, 0, 0, tiled=True)  26.8 us
    dot_general x1, matrix products, local(): lax.dot_general(cols, piece, (((0, 1), (1, 0)), ((), ())), preferred_elem...  25 us
    all_to_all x1, blocking collectives, local(): back = lax.all_to_all(grad_logits, 'tensor', 0, 0, tiled=True)  22.2 us
  transfers between devices with their start and end apart: 5, of which 4 were waited for; matrix products, arithmetic and copies ran while one was open for 8% of the time, Pallas kernels for 0%

profile of v1, /device:TPU:8, one launch (start us, length us, event | category | flops | bytes accessed | tf_op | source)
XLA Modules:
  0.0 471.9 jit_solution(2256680248837307044)
XLA Ops:
  7.2 1.8 reshape_squeeze.12
  9.0 1.6 copy.31
  11.7 1.0 copy.41
  12.7 1.1 fusion.12
  13.7 2.8 rev.3
  16.5 1.4 pad_maximum_fusion.2
  18.0 0.8 stack_reshape.6
  19.0 3.5 copy.25
  22.5 6.3 %all-to-all-start = ((bf16[16,2,32768]{2,1,0:T(2,128)(2,1)}), bf16[16,2,32768]{2,1,0:T(2,128)(2,1)S(1)}, u32[]{:S(2)}, u32[]{:S(2)}) async-start(bf16[16,2,32768]{2,1,0:T(2,128)(2,1)} %copy.25), calls=%async_computation | async-start | bytes 4194304 | tf_op jit(solution)/shard_map/all_to_all | solution.py:35
  28.8 0.7 collective-permute-start
  29.5 26.8 %all-to-all-done = bf16[16,2,32768]{2,1,0:T(2,128)(2,1)S(1)} async-done(((bf16[16,2,32768]{2,1,0:T(2,128)(2,1)}), bf16[16,2,32768]{2,1,0:T(2,128)(2,1)S(1)}, u32[]{:S(2)}, u32[]{:S(2)}) %all-to-all-start) | async-done | bytes 2097184 | tf_op jit(solution)/shard_map/all_to_all | solution.py:35
  56.3 10.0 %slice_reduce_fusion = (bf16[16,32768]{1,0:T(8,128)(2,1)S(1)}, bf16[16,32768]{1,0:T(8,128)(2,1)}) fusion(bf16[16,2,32768]{2,1,0:T(2,128)(2,1)S(1)} %all-to-all-done), kind=kLoop, calls=%fused_computation.9 | loop fusion | bytes 4194304 | tf_op jit(solution)/shard_map/slice | solution.py:36
  66.3 1.8 reshape_squeeze.14
  68.8 11.2 %fusion = f32[512,4096]{1,0:T(8,128)} fusion(bf16[512,1024]{1,0:T(8,128)(2,1)S(1)} %reshape.48, bf16[512,4096]{1,0:T(8,128)(2,1)} %collective-permute-done, bf16[512,4096]{1,0:T(8,128)(2,1)} %param.4), kind=kOutput, calls=%fused_computation | convolution fusion | flops 4311744512 | bytes 17825792 | tf_op jit(solution)/shard_map/dot_general | solution.py:39
  81.3 0.8 dynamic-update-slice
  82.1 29.3 %all-reduce = f32[16]{0:T(128)S(1)} all-reduce(f32[16]{0:T(128)S(1)} %dynamic-update-slice), channel_id=1, replica_groups=mesh['pair'=8,'core'=2,'tensor'=16] {'pair','core'}, use_global_device_ids=true, to_apply=%add | all-reduce | flops 16 | bytes 128 | tf_op jit(solution)/shard_map/optimization_barrier | solution.py:43
  111.4 65.4 %reduce-scatter.3.cloned.1.call-done = f32[64,4096]{1,0:T(8,128)} async-done(((f32[512,4096]{1,0:T(8,128)}), f32[64,4096]{1,0:T(8,128)}) %reduce-scatter.3.cloned.1.call-update) | async-done | bytes 1048592 | tf_op jit(solution)/shard_map/reduce_scatter | solution.py:42
  176.9 1.5 reshape.49
  179.5 1.7 pad_maximum_fusion.1
  181.2 9.5 %all-to-all-start.1 = ((f32[16,5,4096]{2,1,0:T(8,128)}), f32[16,5,4096]{2,1,0:T(8,128)S(1)}, u32[]{:S(2)}, u32[]{:S(2)}) async-start(f32[16,5,4096]{2,1,0:T(8,128)} %pad_maximum_fusion.1), calls=%async_computation.2 | async-start | bytes 4194304 | tf_op jit(solution)/shard_map/all_to_all | solution.py:48
  191.1 51.3 %all-to-all-done.1 = f32[16,5,4096]{2,1,0:T(8,128)S(1)} async-done(((f32[16,5,4096]{2,1,0:T(8,128)}), f32[16,5,4096]{2,1,0:T(8,128)S(1)}, u32[]{:S(2)}, u32[]{:S(2)}) %all-to-all-start.1) | async-done | bytes 1310752 | tf_op jit(solution)/shard_map/all_to_all | solution.py:48
  242.3 1.1 fusion.11
  243.5 1.8 exponential_reduce_fusion.1
  247.2 0.7 exponential_reduce_fusion
  248.5 2.2 multiply_reduce_fusion
  251.4 22.2 %all_to_all.20 = bf16[16,4,4096]{2,1,0:T(4,128)(2,1)S(1)} all-to-all(bf16[16,4,4096]{2,1,0:T(4,128)(2,1)S(1)} %multiply_convert_fusion), channel_id=1, replica_groups=mesh['pair'=8,'core'=2,'tensor'=16] {'tensor'}, dimensions={0} | all-to-all | bytes 1048576 | tf_op jit(solution)/shard_map/all_to_all | solution.py:60
  273.7 1.0 stack.11
  274.7 97.8 %all_to_all.21 = bf16[16,4,16,4096]{3,2,1,0:T(8,128)(2,1)S(1)} all-to-all(bf16[16,4,16,4096]{3,2,1,0:T(8,128)(2,1)S(1)} %stack.11), channel_id=1, replica_groups=mesh['pair'=8,'core'=2,'tensor'=16] {'pair','core'}, dimensions={0} | all-to-all | bytes 16777216 | tf_op jit(solution)/shard_map/all_to_all | solution.py:63
  372.5 4.5 fusion.8
  377.1 2.6 copy.28
  380.0 25.0 %bitcast_convert_fusion = bf16[512,4096]{1,0:T(8,128)(2,1)} fusion(bf16[16,64,512]{2,1,0:T(8,128)(2,1)S(1)} %bitcast.41, bf16[64,16,4096]{2,1,0:T(8,128)(2,1)} %bitcast.32), kind=kOutput, calls=%fused_computation.4 | convolution fusion | flops 4297064448 | bytes 13631488 | tf_op jit(solution)/shard_map/dot_general | solution.py:64
  405.0 59.8 %reduce-scatter.5.cloned.1.call-done = f32[64,1,512]{2,0,1:T(8,128)} async-done(((f32[64,16,512]{2,0,1:T(8,128)}), f32[64,1,512]{2,0,1:T(8,128)}) %reduce-scatter.5.cloned.1.call-update) | async-done | bytes 131088 | tf_op jit(solution)/shard_map/reduce_scatter | solution.py:70
  (30 shorter events, 6.2 us)
Async XLA Ops:
  22.5 33.8 %all-to-all-start = ((bf16[16,2,32768]{2,1,0:T(2,128)(2,1)}), bf16[16,2,32768]{2,1,0:T(2,128)(2,1)S(1)}, u32[]{:S(2)}, u32[]{:S(2)}) async-start(bf16[16,2,32768]{2,1,0:T(2,128)(2,1)} %copy.25), calls=%async_computation | async-start | bytes 4194304 | tf_op jit(solution)/shard_map/all_to_all | solution.py:35
  28.8 148.1 %reduce-scatter.3.cloned.1.call-start = ((), (), s32[]{:S(2)}) async-start(), calls=%async_computation.6 | async-start | bytes 9437184 | tf_op jit(solution)/shard_map/reduce_scatter | solution.py:42
  28.8 40.0 %collective-permute-start = (bf16[512,4096]{1,0:T(8,128)(2,1)}, bf16[512,4096]{1,0:T(8,128)(2,1)}, u32[]{:S(2)}, u32[]{:S(2)}) collective-permute-start(bf16[512,4096]{1,0:T(8,128)(2,1)} %param.4), channel_id=1, source_target_pairs={{0,16},{16,0},{1,17},{17,1},{2,18},{18,2},{3,19},{19,3},{4,20},{20... | collective-permute-start | bytes 12582920 | tf_op jit(solution)/shard_map/ppermute | solution.py:28
  80.0 0.7 copy-start.2
  181.2 61.1 %all-to-all-start.1 = ((f32[16,5,4096]{2,1,0:T(8,128)}), f32[16,5,4096]{2,1,0:T(8,128)S(1)}, u32[]{:S(2)}, u32[]{:S(2)}) async-start(f32[16,5,4096]{2,1,0:T(8,128)} %pad_maximum_fusion.1), calls=%async_computation.2 | async-start | bytes 4194304 | tf_op jit(solution)/shard_map/all_to_all | solution.py:48
  190.8 274.1 %reduce-scatter.5.cloned.1.call-start = ((), (), s32[]{:S(2)}) async-start(), calls=%async_computation.7 | async-start | bytes 2228224 | tf_op jit(solution)/shard_map/reduce_scatter | solution.py:70
  274.7 97.8 %copy-start.1 = (bf16[512,4096]{1,0:T(8,128)(2,1)S(1)}, bf16[512,4096]{1,0:T(8,128)(2,1)}, u32[]{:S(2)}) copy-start(bf16[512,4096]{1,0:T(8,128)(2,1)} %param.4) | copy-start | bytes 12582916
  372.5 4.5 copy-start
Sparse Core Ops, SparseCore 0:
  80.2 96.6 reduce-scatter.2
  379.8 85.0 reduce-scatter.4
